TPU v7x, 32 devices: a whole 2x2x4 slice. The times are simulated.
32 devices in a mesh: chain: 2 (over x), ops: 8 (over z, y), sector: 2 (over core).
Axes of the slice: x: 2, y: 2, z: 4, core: 2. Of those that a mesh axis runs over, the one named last changes fastest.
Arguments:
- psi: bfloat16 [2, 8, 384, 384], P('chain', 'sector'), may hold values from -90 to 90
- left_ops: bfloat16 [2, 96, 8, 384, 384], P('chain', 'ops', 'sector'), may hold values from -1 to 2
- right_ops: bfloat16 [2, 96, 8, 384, 384], P('chain', 'ops', 'sector'), may hold values from -1 to 1
- basis: bfloat16 [2, 8, 384, 384], P('chain', 'sector'), may hold values from -0.3125 to 0.3125
- block_dims: int32 [2, 8], P('chain', 'sector'), may hold values from 64 to 384, as said below
Outputs:
- residual: float32 [2, 8, 384, 384], P('chain', 'sector', 'ops')
- thetas: float32 [2, 3], P('chain')
Inputs may be any that keep to these rules, and one draw needn't show every extreme that they name: `block_dims`: each is a multiple of 64; every section has a sector of exactly 384.
All inputs are finite; a program needn't handle non-finite values.
Results may differ from a plain program's by a relative error of at most 0.009.
Values may be sent and summed in bfloat16 or wider, within the bound.
No kernel may reach another device: no remote copies, remote signals or barrier semaphores. Data moves between devices by JAX's collectives and lax.ppermute only.
A program may use at most 128 MiB of HBM per device.

v0:
```python
import jax
import jax.numpy as jnp
from jax import lax
from jax.sharding import PartitionSpec as P

SECTORS = 8
ITERS = 3


def from_behind(block, axis, distance):
    devices = range(lax.axis_size(axis))
    route = [((i - distance) % len(devices), i) for i in devices]
    return lax.ppermute(block, axis, route)


def live_mask(block_dims, block_size):
    index_rows = jnp.arange(block_size, dtype=jnp.int32)
    limits = block_dims[:, :, None, None]
    inside = (index_rows[None, None, :, None] < limits) & (index_rows[None, None, None, :] < limits)
    return inside.astype(jnp.float32)


def quotient(vector_rows, sigma_rows):
    correlation, norm_sum = lax.psum(
        (jnp.sum(vector_rows * sigma_rows), jnp.sum(vector_rows * vector_rows)), ("ops", "sector")
    )
    rayleigh = correlation / norm_sum
    leftover = sigma_rows - rayleigh * vector_rows
    spread = lax.psum(jnp.sum(leftover * leftover), ("ops", "sector"))
    return (rayleigh, spread)


def on_device(psi, left_ops, right_ops, basis, block_dims):
    block_size = psi.shape[2]
    live = live_mask(block_dims, block_size)
    half_env = jnp.einsum(
        "ckqab,cqbd->ckqad", left_ops, basis, preferred_element_type=jnp.float32
    ).astype(jnp.bfloat16)
    boundary_ops = jnp.einsum(
        "cqba,ckqbd->ckqad", basis, half_env, preferred_element_type=jnp.float32
    ).astype(jnp.bfloat16)
    shifted = from_behind(boundary_ops, "chain", 1)
    vector = jnp.where(live > 0, psi, jnp.zeros_like(psi))
    entry_count = float(SECTORS * block_size * block_size)
    share_rows = block_size // lax.axis_size("ops")
    row_start = lax.axis_index("ops") * share_rows
    live_rows = lax.dynamic_slice_in_dim(live, row_start, share_rows, 2)
    residual = jnp.zeros(live_rows.shape, jnp.float32)
    quotients = []
    for iteration in range(ITERS):
        products = jnp.einsum(
            "ckqab,cqbd->ckqad", shifted, vector, preferred_element_type=jnp.float32
        ).astype(jnp.bfloat16)
        partial_sigma = jnp.einsum(
            "ckqad,ckqed->cqae", products, right_ops, preferred_element_type=jnp.float32
        )
        sigma_full = lax.psum(partial_sigma, "ops") * live
        sigma_rows = lax.dynamic_slice_in_dim(sigma_full, row_start, share_rows, 2)
        vector_rows = lax.dynamic_slice_in_dim(vector, row_start, share_rows, 2).astype(jnp.float32)
        rayleigh, spread = quotient(vector_rows, sigma_rows)
        quotients.append(rayleigh)
        if iteration + 1 < ITERS:
            residue = sigma_full - rayleigh * vector.astype(jnp.float32)
            vector = (residue * lax.rsqrt(spread / entry_count + 1e-06)).astype(jnp.bfloat16)
        else:
            residual = sigma_rows - rayleigh * vector_rows
    thetas = jnp.stack(quotients).reshape(1, ITERS)
    return (residual, thetas)


def solution(mesh):
    in_specs = (
        P("chain", "sector", None, None),
        P("chain", "ops", "sector", None, None),
        P("chain", "ops", "sector", None, None),
        P("chain", "sector", None, None),
        P("chain", "sector"),
    )
    out_specs = (P("chain", "sector", "ops", None), P("chain", None))
    return jax.shard_map(
        on_device, mesh=mesh, in_specs=in_specs, out_specs=out_specs, check_vma=False
    )
```

profile of v0, /device:TPU:0, one launch (start us, length us, event | category | flops | bytes accessed | tf_op | source)
XLA Modules:
  0.0 908.4 jit_solution(11232983917351738065)
XLA Ops:
  7.2 0.0 copy-start
  7.2 0.0 copy-start.7
  7.2 0.0 copy-start.4
  7.2 0.0 all-reduce.7.cloned.1.call-start
  7.2 1.2 copy-done
  8.4 21.1 %convert_bitcast_fusion = bf16[1,12,4,384,384]{3,4,1,2,0:T(8,128)(2,1)} fusion(bf16[1,4,384,384]{3,2,1,0:T(8,128)(2,1)S(1)} %copy-done, bf16[1,12,4,384,384]{4,3,2,1,0:T(8,128)(2,1)} %param.6), kind=kOutput, calls=%fused_computation.19 | convolution fusion | flops 10885791744 | bytes 29491200 | tf_op jit(solution)/shard_map/cqba,ckqbd->ckqad/dot_general | solution.py:39
  29.5 2.9 collective-permute-start
  32.4 0.0 copy-done.7
  32.4 0.1 iota_compare_fusion
  32.5 0.0 copy-done.4
  32.5 0.5 fusion.43
  33.0 303.8 %collective-permute-done = bf16[1,12,4,384,384]{3,4,1,2,0:T(8,128)(2,1)} collective-permute-done((bf16[1,12,4,384,384]{3,4,1,2,0:T(8,128)(2,1)}, bf16[1,12,4,384,384]{3,4,1,2,0:T(8,128)(2,1)}, u32[]{:S(2)}, u32[]{:S(2)}) %collective-permute-start) | collective-permute-done | bytes 14155808 | tf_op jit(solution)/shard_map/ppermute | solution.py:13
  336.8 20.1 %fusion.44 = f32[1,4,384,384]{3,2,1,0:T(8,128)} fusion(bf16[1,12,4,384,384]{3,4,1,2,0:T(8,128)(2,1)} %collective-permute-done, bf16[1,4,384,384]{3,2,1,0:T(8,128)(2,1)S(1)} %fusion.43, bf16[1,12,4,384,384]{4,3,2,1,0:T(8,128)(2,1)} %param.7), kind=kOutput, calls=%fused_computation.30 | convolution fusion | flops 10878713856 | bytes 31850496 | tf_op jit(solution)/shard_map/ckqad,ckqed->cqae/dot_general | solution.py:54
  356.9 0.0 all-reduce.7.cloned.1.call-update
  357.0 0.0 all-reduce.9.cloned.1.call-start
  357.0 110.3 %all-reduce.7.cloned.1.call-done = f32[1,4,384,384]{3,2,1,0:T(8,128)} async-done(((f32[1,4,384,384]{3,2,1,0:T(8,128)}), f32[1,4,384,384]{3,2,1,0:T(8,128)}) %all-reduce.7.cloned.1.call-update) | async-done | bytes 2359312 | tf_op jit(solution)/shard_map/psum | solution.py:57
  467.4 0.0 copy-start.2
  467.4 2.1 and_select_fusion.1
  469.5 0.0 copy-start.5
  469.5 1.4 copy-done.5
  470.9 0.7 fusion.74
  471.6 32.1 %all-reduce.2 = (f32[]{:T(128)}, f32[]{:T(128)}) all-reduce(f32[]{:T(128)} %get-tuple-element.7, f32[]{:T(128)} %get-tuple-element.6), channel_id=1, replica_groups=mesh['chain'=2,'ops'=8,'sector'=2] {'ops','sector'}, use_global_device_ids=true, to_apply=%region_2.3 | all-reduce | flops 2 | bytes 16 | tf_op jit(solution)/shard_map/psum | solution.py:24
  505.0 1.7 fusion.77
  506.7 30.3 %psum.80 = f32[]{:T(128)} all-reduce(f32[]{:T(128)} %fusion.77), channel_id=1, replica_groups=mesh['chain'=2,'ops'=8,'sector'=2] {'ops','sector'}, use_global_device_ids=true, to_apply=%region_6.7 | all-reduce | flops 1 | bytes 8 | tf_op jit(solution)/shard_map/psum | solution.py:29
  537.6 0.0 copy-done.2
  537.7 2.1 multiply_convert_fusion.1
  539.7 20.1 %fusion.51 = f32[1,4,384,384]{3,2,1,0:T(8,128)} fusion(bf16[1,12,4,384,384]{3,4,1,2,0:T(8,128)(2,1)} %collective-permute-done, bf16[1,4,384,384]{3,2,1,0:T(8,128)(2,1)S(1)} %multiply_convert_fusion.1, bf16[1,12,4,384,384]{4,3,2,1,0:T(8,128)(2,1)} %param.7), kind=kOutput, calls=%fused_computation.31 | convolution fusion | flops 10878713856 | bytes 31850496 | tf_op jit(solution)/shard_map/ckqad,ckqed->cqae/dot_general | solution.py:54
  559.9 0.0 all-reduce.9.cloned.1.call-update
  559.9 0.0 all-reduce.11.cloned.1.call-start
  559.9 106.1 %all-reduce.9.cloned.1.call-done = f32[1,4,384,384]{3,2,1,0:T(8,128)} async-done(((f32[1,4,384,384]{3,2,1,0:T(8,128)}), f32[1,4,384,384]{3,2,1,0:T(8,128)}) %all-reduce.9.cloned.1.call-update) | async-done | bytes 2359312 | tf_op jit(solution)/shard_map/psum | solution.py:57
  666.0 0.0 copy-start.3
  666.0 2.1 and_select_fusion
  668.1 0.0 copy-start.6
  668.1 1.4 copy-done.6
  669.6 0.7 fusion.79
  670.3 32.1 %all-reduce.1 = (f32[]{:T(128)}, f32[]{:T(128)}) all-reduce(f32[]{:T(128)} %get-tuple-element.5, f32[]{:T(128)} %get-tuple-element.4), channel_id=1, replica_groups=mesh['chain'=2,'ops'=8,'sector'=2] {'ops','sector'}, use_global_device_ids=true, to_apply=%region_9.10 | all-reduce | flops 2 | bytes 16 | tf_op jit(solution)/shard_map/psum | solution.py:24
  703.7 1.7 fusion.82
  705.3 30.1 %psum.84 = f32[]{:T(128)} all-reduce(f32[]{:T(128)} %fusion.82), channel_id=1, replica_groups=mesh['chain'=2,'ops'=8,'sector'=2] {'ops','sector'}, use_global_device_ids=true, to_apply=%region_13.14 | all-reduce | flops 1 | bytes 8 | tf_op jit(solution)/shard_map/psum | solution.py:29
  736.1 0.0 copy-done.3
  736.1 1.7 multiply_convert_fusion
  737.8 0.0 copy-start.1
  737.8 20.3 %fusion.58 = f32[1,4,384,384]{3,2,1,0:T(8,128)} fusion(bf16[1,12,4,384,384]{3,4,1,2,0:T(8,128)(2,1)} %collective-permute-done, bf16[1,4,384,384]{3,2,1,0:T(8,128)(2,1)} %multiply_convert_fusion, bf16[1,12,4,384,384]{4,3,2,1,0:T(8,128)(2,1)} %param.7), kind=kOutput, calls=%fused_computation.32 | convolution fusion | flops 10878713856 | bytes 31850496 | tf_op jit(solution)/shard_map/ckqad,ckqed->cqae/dot_general | solution.py:54
  758.1 0.0 all-reduce.11.cloned.1.call-update
  758.1 0.3 broadcast_and_fusion
  758.5 105.7 %all-reduce.11.cloned.1.call-done = f32[1,4,384,384]{3,2,1,0:T(8,128)} async-done(((f32[1,4,384,384]{3,2,1,0:T(8,128)}), f32[1,4,384,384]{3,2,1,0:T(8,128)}) %all-reduce.11.cloned.1.call-update) | async-done | bytes 2359312 | tf_op jit(solution)/shard_map/psum | solution.py:57
  864.2 1.8 fusion.84
  866.0 32.2 %all-reduce = (f32[]{:T(128)}, f32[]{:T(128)}) all-reduce(f32[]{:T(128)} %get-tuple-element.3, f32[]{:T(128)} %get-tuple-element.2), channel_id=1, replica_groups=mesh['chain'=2,'ops'=8,'sector'=2] {'ops','sector'}, use_global_device_ids=true, to_apply=%region_16.17 | all-reduce | flops 2 | bytes 16 | tf_op jit(solution)/shard_map/psum | solution.py:24
  899.5 0.6 maximum_bitcast_fusion
  900.1 1.8 fusion.85
  901.9 0.0 copy-done.1
Async XLA Ops:
  7.2 1.3 copy-start
  7.2 25.3 %copy-start.7 = (s32[1,4]{1,0:T(1,128)S(1)}, s32[1,4]{1,0:T(1,128)}, u32[]{:S(2)}) copy-start(s32[1,4]{1,0:T(1,128)} %param.9) | copy-start | bytes 52
  7.2 25.3 %copy-start.4 = (bf16[1,4,384,384]{3,2,1,0:T(8,128)(2,1)S(1)}, bf16[1,4,384,384]{3,2,1,0:T(8,128)(2,1)}, u32[]{:S(2)}) copy-start(bf16[1,4,384,384]{3,2,1,0:T(8,128)(2,1)} %param.5) | copy-start | bytes 3538948
  7.2 460.2 %all-reduce.7.cloned.1.call-start = ((), (), s32[]{:S(2)}) async-start(), calls=%async_computation | async-start | bytes 4718592 | tf_op jit(solution)/shard_map/psum | solution.py:57
  29.5 307.3 %collective-permute-start = (bf16[1,12,4,384,384]{3,4,1,2,0:T(8,128)(2,1)}, bf16[1,12,4,384,384]{3,4,1,2,0:T(8,128)(2,1)}, u32[]{:S(2)}, u32[]{:S(2)}) collective-permute-start(bf16[1,12,4,384,384]{3,4,1,2,0:T(8,128)(2,1)} %convert_bitcast_fusion), channel_id=1, source_target_pairs={{16,0},{0,16},{17,1},{1,17},{18,2},{2,18},{19,3},{3,19},{20,4},{4,... | collective-permute-start | bytes 42467336 | tf_op jit(solution)/shard_map/ppermute | solution.py:13
  357.0 309.0 %all-reduce.9.cloned.1.call-start = ((), (), s32[]{:S(2)}) async-start(), calls=%async_computation.1 | async-start | bytes 4718592 | tf_op jit(solution)/shard_map/psum | solution.py:57
  467.4 70.3 %copy-start.2 = (f32[1,4,384,384]{3,2,1,0:T(8,128)S(1)}, f32[1,4,384,384]{3,2,1,0:T(8,128)}, u32[]{:S(2)}) copy-start(f32[1,4,384,384]{3,2,1,0:T(8,128)} %all-reduce.7.cloned.1.call-done) | copy-start | bytes 7077892
  469.5 1.4 copy-start.5
  559.9 304.3 %all-reduce.11.cloned.1.call-start = ((), (), s32[]{:S(2)}) async-start(), calls=%async_computation.2 | async-start | bytes 4718592 | tf_op jit(solution)/shard_map/psum | solution.py:57
  666.0 70.1 %copy-start.3 = (f32[1,4,384,384]{3,2,1,0:T(8,128)S(1)}, f32[1,4,384,384]{3,2,1,0:T(8,128)}, u32[]{:S(2)}) copy-start(f32[1,4,384,384]{3,2,1,0:T(8,128)} %all-reduce.9.cloned.1.call-done) | copy-start | bytes 7077892
  668.1 1.4 copy-start.6
  737.8 164.1 %copy-start.1 = (bf16[1,4,384,384]{3,2,1,0:T(8,128)(2,1)S(1)}, bf16[1,4,384,384]{3,2,1,0:T(8,128)(2,1)}, u32[]{:S(2)}) copy-start(bf16[1,4,384,384]{3,2,1,0:T(8,128)(2,1)} %param.8) | copy-start | bytes 3538948
Sparse Core Ops, SparseCore 0:
  357.1 110.2 all-reduce.6
  560.0 105.9 all-reduce.8
  758.3 105.8 all-reduce.10
where the time goes:
time: 909 us; the launch traced here: 908 us
  waiting for transfers between devices  626 us (69%)
  blocking collectives  157 us (17%)
  matrix products  81.7 us (9%)
  between operations  19.3 us (2%)
  other arithmetic  17.8 us (2%)
    psum x3, waiting for transfers between devices, on_device(): sigma_full = lax.psum(partial_sigma, 'ops') * live  322 us
    ppermute x1, waiting for transfers between devices, from_behind(): return lax.ppermute(block, axis, route)  304 us
    psum x3, blocking collectives, quotient(): lax.psum((jnp.sum(vector_rows * sigma_rows), jnp.sum(vector_rows * vector...  96.3 us
    dot_general x3, matrix products, on_device(): jnp.einsum('ckqad,ckqed->cqae', products, right_ops, preferred_element_ty...  60.6 us
    psum x2, blocking collectives, quotient(): spread = lax.psum(jnp.sum(leftover * leftover), ('ops', 'sector'))  60.4 us
    dot_general x1, matrix products, on_device(): jnp.einsum('cqba,ckqbd->ckqad', basis, half_env, preferred_element_type=j...  21.1 us
  transfers between devices with their start and end apart: 4, of which 4 were waited for; matrix products, arithmetic and copies ran while one was open for 0% of the time, Pallas kernels for 0%

commit v1 on v0

--- a/solution.py
+++ b/solution.py
@@ -5,6 +5,7 @@
 
 SECTORS = 8
 ITERS = 3
+connect_samples = lambda xs: jax.lax.psum(jax.lax.psum(xs, "sector"), "ops")
 
 
 def from_behind(block, axis, distance):
@@ -21,8 +22,8 @@
 
 
 def quotient(vector_rows, sigma_rows):
-    correlation, norm_sum = lax.psum(
-        (jnp.sum(vector_rows * sigma_rows), jnp.sum(vector_rows * vector_rows)), ("ops", "sector")
+    correlation, norm_sum = connect_samples(
+        (jnp.sum(vector_rows * sigma_rows), jnp.sum(vector_rows * vector_rows))
     )
     rayleigh = correlation / norm_sum
     leftover = sigma_rows - rayleigh * vector_rows

time: 909 us -> 882 us (0.970)
  blocking collectives: 157 us -> 130 us
    psum x3 -> x6, blocking collectives: 96.3 us -> 69.7 us  [connect_samples = lambda xs: jax.lax.psum(jax.lax.psum(xs, 'sector'), 'ops')]
where the time goes in v1:
time: 882 us
  waiting for transfers between devices  626 us (71%)
  blocking collectives  130 us (15%)
  matrix products  81.7 us (9%)
  between operations  19.3 us (2%)
  other arithmetic  17.8 us (2%)
    psum x3, waiting for transfers between devices, on_device(): sigma_full = lax.psum(partial_sigma, 'ops') * live  322 us
    ppermute x1, waiting for transfers between devices, from_behind(): return lax.ppermute(block, axis, route)  304 us
    psum x6, blocking collectives, connect_samples = lambda xs: jax.lax.psum(jax.lax.psum(xs, 'sector'), 'ops')  69.7 us
    dot_general x3, matrix products, on_device(): jnp.einsum('ckqad,ckqed->cqae', products, right_ops, preferred_element_ty...  60.6 us
    psum x2, blocking collectives, quotient(): spread = lax.psum(jnp.sum(leftover * leftover), ('ops', 'sector'))  60.4 us
    dot_general x1, matrix products, on_device(): jnp.einsum('cqba,ckqbd->ckqad', basis, half_env, preferred_element_type=j...  21.1 us
  transfers between devices with their start and end apart: 4, of which 4 were waited for; matrix products, arithmetic and copies ran while one was open for 0% of the time, Pallas kernels for 0%

profile of v1, /device:TPU:0, one launch (start us, length us, event | category | flops | bytes accessed | tf_op | source)
XLA Modules:
  0.0 881.8 jit_solution(12792004924860882568)
XLA Ops:
  7.2 0.0 copy-start
  7.2 0.0 copy-start.7
  7.2 0.0 copy-start.4
  7.2 0.0 all-reduce.10.cloned.1.call-start
  7.2 1.2 copy-done
  8.4 21.1 %convert_bitcast_fusion = bf16[1,12,4,384,384]{3,4,1,2,0:T(8,128)(2,1)} fusion(bf16[1,4,384,384]{3,2,1,0:T(8,128)(2,1)S(1)} %copy-done, bf16[1,12,4,384,384]{4,3,2,1,0:T(8,128)(2,1)} %param.6), kind=kOutput, calls=%fused_computation.19 | convolution fusion | flops 10885791744 | bytes 29491200 | tf_op jit(solution)/shard_map/cqba,ckqbd->ckqad/dot_general | solution.py:40
  29.5 2.9 collective-permute-start
  32.4 0.0 copy-done.7
  32.4 0.1 iota_compare_fusion
  32.5 0.0 copy-done.4
  32.5 0.5 fusion.43
  33.0 303.8 %collective-permute-done = bf16[1,12,4,384,384]{3,4,1,2,0:T(8,128)(2,1)} collective-permute-done((bf16[1,12,4,384,384]{3,4,1,2,0:T(8,128)(2,1)}, bf16[1,12,4,384,384]{3,4,1,2,0:T(8,128)(2,1)}, u32[]{:S(2)}, u32[]{:S(2)}) %collective-permute-start) | collective-permute-done | bytes 14155808 | tf_op jit(solution)/shard_map/ppermute | solution.py:14
  336.8 20.1 %fusion.44 = f32[1,4,384,384]{3,2,1,0:T(8,128)} fusion(bf16[1,12,4,384,384]{3,4,1,2,0:T(8,128)(2,1)} %collective-permute-done, bf16[1,4,384,384]{3,2,1,0:T(8,128)(2,1)S(1)} %fusion.43, bf16[1,12,4,384,384]{4,3,2,1,0:T(8,128)(2,1)} %param.7), kind=kOutput, calls=%fused_computation.30 | convolution fusion | flops 10878713856 | bytes 31850496 | tf_op jit(solution)/shard_map/ckqad,ckqed->cqae/dot_general | solution.py:55
  356.9 0.0 all-reduce.10.cloned.1.call-update
  357.0 0.0 all-reduce.12.cloned.1.call-start
  357.0 110.3 %all-reduce.10.cloned.1.call-done = f32[1,4,384,384]{3,2,1,0:T(8,128)} async-done(((f32[1,4,384,384]{3,2,1,0:T(8,128)}), f32[1,4,384,384]{3,2,1,0:T(8,128)}) %all-reduce.10.cloned.1.call-update) | async-done | bytes 2359312 | tf_op jit(solution)/shard_map/psum | solution.py:58
  467.4 0.0 copy-start.2
  467.4 2.1 and_select_fusion.1
  469.5 0.0 copy-start.5
  469.5 1.4 copy-done.5
  470.9 0.7 fusion.74
  471.6 3.1 all-reduce.5
  474.7 20.1 %all-reduce.2 = (f32[]{:T(128)}, f32[]{:T(128)}) all-reduce(f32[]{:T(128)} %get-tuple-element.18, f32[]{:T(128)} %get-tuple-element.19), channel_id=1, replica_groups=mesh['chain'=2,'ops'=8,'sector'=2] {'ops'}, use_global_device_ids=true, to_apply=%region_3.4 | all-reduce | flops 2 | bytes 16 | tf_op jit(solution)/shard_map/psum | solution.py:8
  496.1 1.7 fusion.77
  497.8 30.3 %psum.124 = f32[]{:T(128)} all-reduce(f32[]{:T(128)} %fusion.77), channel_id=1, replica_groups=mesh['chain'=2,'ops'=8,'sector'=2] {'ops','sector'}, use_global_device_ids=true, to_apply=%region_8.9 | all-reduce | flops 1 | bytes 8 | tf_op jit(solution)/shard_map/psum | solution.py:30
  528.8 0.0 copy-done.2
  528.8 2.1 multiply_convert_fusion.1
  530.8 20.1 %fusion.51 = f32[1,4,384,384]{3,2,1,0:T(8,128)} fusion(bf16[1,12,4,384,384]{3,4,1,2,0:T(8,128)(2,1)} %collective-permute-done, bf16[1,4,384,384]{3,2,1,0:T(8,128)(2,1)S(1)} %multiply_convert_fusion.1, bf16[1,12,4,384,384]{4,3,2,1,0:T(8,128)(2,1)} %param.7), kind=kOutput, calls=%fused_computation.31 | convolution fusion | flops 10878713856 | bytes 31850496 | tf_op jit(solution)/shard_map/ckqad,ckqed->cqae/dot_general | solution.py:55
  551.0 0.0 all-reduce.12.cloned.1.call-update
  551.0 0.0 all-reduce.14.cloned.1.call-start
  551.1 106.0 %all-reduce.12.cloned.1.call-done = f32[1,4,384,384]{3,2,1,0:T(8,128)} async-done(((f32[1,4,384,384]{3,2,1,0:T(8,128)}), f32[1,4,384,384]{3,2,1,0:T(8,128)}) %all-reduce.12.cloned.1.call-update) | async-done | bytes 2359312 | tf_op jit(solution)/shard_map/psum | solution.py:58
  657.1 0.0 copy-start.3
  657.1 2.1 and_select_fusion
  659.2 0.0 copy-start.6
  659.2 1.4 copy-done.6
  660.6 0.7 fusion.79
  661.3 3.1 all-reduce.4
  664.5 20.1 %all-reduce.1 = (f32[]{:T(128)}, f32[]{:T(128)}) all-reduce(f32[]{:T(128)} %get-tuple-element.16, f32[]{:T(128)} %get-tuple-element.17), channel_id=1, replica_groups=mesh['chain'=2,'ops'=8,'sector'=2] {'ops'}, use_global_device_ids=true, to_apply=%region_12.13 | all-reduce | flops 2 | bytes 16 | tf_op jit(solution)/shard_map/psum | solution.py:8
  685.9 1.7 fusion.82
  687.5 30.1 %psum.130 = f32[]{:T(128)} all-reduce(f32[]{:T(128)} %fusion.82), channel_id=1, replica_groups=mesh['chain'=2,'ops'=8,'sector'=2] {'ops','sector'}, use_global_device_ids=true, to_apply=%region_17.18 | all-reduce | flops 1 | bytes 8 | tf_op jit(solution)/shard_map/psum | solution.py:30
  718.3 0.0 copy-done.3
  718.3 1.7 multiply_convert_fusion
  720.0 0.0 copy-start.1
  720.0 20.3 %fusion.58 = f32[1,4,384,384]{3,2,1,0:T(8,128)} fusion(bf16[1,12,4,384,384]{3,4,1,2,0:T(8,128)(2,1)} %collective-permute-done, bf16[1,4,384,384]{3,2,1,0:T(8,128)(2,1)} %multiply_convert_fusion, bf16[1,12,4,384,384]{4,3,2,1,0:T(8,128)(2,1)} %param.7), kind=kOutput, calls=%fused_computation.32 | convolution fusion | flops 10878713856 | bytes 31850496 | tf_op jit(solution)/shard_map/ckqad,ckqed->cqae/dot_general | solution.py:55
  740.3 0.0 all-reduce.14.cloned.1.call-update
  740.3 0.3 broadcast_and_fusion
  740.7 105.7 %all-reduce.14.cloned.1.call-done = f32[1,4,384,384]{3,2,1,0:T(8,128)} async-done(((f32[1,4,384,384]{3,2,1,0:T(8,128)}), f32[1,4,384,384]{3,2,1,0:T(8,128)}) %all-reduce.14.cloned.1.call-update) | async-done | bytes 2359312 | tf_op jit(solution)/shard_map/psum | solution.py:58
  846.4 1.8 fusion.84
  848.2 3.1 all-reduce.3
  851.4 20.2 %all-reduce = (f32[]{:T(128)}, f32[]{:T(128)}) all-reduce(f32[]{:T(128)} %get-tuple-element.14, f32[]{:T(128)} %get-tuple-element.15), channel_id=1, replica_groups=mesh['chain'=2,'ops'=8,'sector'=2] {'ops'}, use_global_device_ids=true, to_apply=%region_21.22 | all-reduce | flops 2 | bytes 16 | tf_op jit(solution)/shard_map/psum | solution.py:8
  872.9 0.6 maximum_bitcast_fusion
  873.5 1.8 fusion.85
  875.3 0.0 copy-done.1
Async XLA Ops:
  7.2 1.3 copy-start
  7.2 25.3 %copy-start.7 = (s32[1,4]{1,0:T(1,128)S(1)}, s32[1,4]{1,0:T(1,128)}, u32[]{:S(2)}) copy-start(s32[1,4]{1,0:T(1,128)} %param.9) | copy-start | bytes 52
  7.2 25.3 %copy-start.4 = (bf16[1,4,384,384]{3,2,1,0:T(8,128)(2,1)S(1)}, bf16[1,4,384,384]{3,2,1,0:T(8,128)(2,1)}, u32[]{:S(2)}) copy-start(bf16[1,4,384,384]{3,2,1,0:T(8,128)(2,1)} %param.5) | copy-start | bytes 3538948
  7.2 460.2 %all-reduce.10.cloned.1.call-start = ((), (), s32[]{:S(2)}) async-start(), calls=%async_computation | async-start | bytes 4718592 | tf_op jit(solution)/shard_map/psum | solution.py:58
  29.5 307.3 %collective-permute-start = (bf16[1,12,4,384,384]{3,4,1,2,0:T(8,128)(2,1)}, bf16[1,12,4,384,384]{3,4,1,2,0:T(8,128)(2,1)}, u32[]{:S(2)}, u32[]{:S(2)}) collective-permute-start(bf16[1,12,4,384,384]{3,4,1,2,0:T(8,128)(2,1)} %convert_bitcast_fusion), channel_id=1, source_target_pairs={{16,0},{0,16},{17,1},{1,17},{18,2},{2,18},{19,3},{3,19},{20,4},{4,... | collective-permute-start | bytes 42467336 | tf_op jit(solution)/shard_map/ppermute | solution.py:14
  357.0 300.1 %all-reduce.12.cloned.1.call-start = ((), (), s32[]{:S(2)}) async-start(), calls=%async_computation.1 | async-start | bytes 4718592 | tf_op jit(solution)/shard_map/psum | solution.py:58
  467.4 61.4 %copy-start.2 = (f32[1,4,384,384]{3,2,1,0:T(8,128)S(1)}, f32[1,4,384,384]{3,2,1,0:T(8,128)}, u32[]{:S(2)}) copy-start(f32[1,4,384,384]{3,2,1,0:T(8,128)} %all-reduce.10.cloned.1.call-done) | copy-start | bytes 7077892
  469.5 1.4 copy-start.5
  551.0 295.4 %all-reduce.14.cloned.1.call-start = ((), (), s32[]{:S(2)}) async-start(), calls=%async_computation.2 | async-start | bytes 4718592 | tf_op jit(solution)/shard_map/psum | solution.py:58
  657.1 61.2 %copy-start.3 = (f32[1,4,384,384]{3,2,1,0:T(8,128)S(1)}, f32[1,4,384,384]{3,2,1,0:T(8,128)}, u32[]{:S(2)}) copy-start(f32[1,4,384,384]{3,2,1,0:T(8,128)} %all-reduce.12.cloned.1.call-done) | copy-start | bytes 7077892
  659.2 1.4 copy-start.6
  720.0 155.3 %copy-start.1 = (bf16[1,4,384,384]{3,2,1,0:T(8,128)(2,1)S(1)}, bf16[1,4,384,384]{3,2,1,0:T(8,128)(2,1)}, u32[]{:S(2)}) copy-start(bf16[1,4,384,384]{3,2,1,0:T(8,128)(2,1)} %param.8) | copy-start | bytes 3538948
Sparse Core Ops, SparseCore 0:
  357.1 110.2 all-reduce.9
  551.1 105.9 all-reduce.11
  740.5 105.9 all-reduce.13
